TPU v7x, 128 devices: a whole 4x4x4 slice. The times are simulated.
128 devices in a mesh: layer: 16 (over y, x), prow: 4 (over z), pcol: 2 (over core).
Axes of the slice: x: 4, y: 4, z: 4, core: 2. Of those that a mesh axis runs over, the one named last changes fastest.
Arguments:
- front: bfloat16 [16, 2048, 32768], P('layer', 'prow', 'pcol'), may hold values from -6 to 6
- pivots: bfloat16 [16, 2, 256, 32768], P('layer', None, 'prow', 'pcol'), may hold values from -0.8984375 to 0.8984375
- inverses: bfloat16 [16, 2, 256, 256], P('layer'), may hold values from -0.1875 to 0.1875
- slab_pattern: int32 [16, 8, 128], P('layer', 'prow', 'pcol'), may hold values 0 or 1
- pivot_pattern: int32 [16, 2, 128], P('layer', None, 'pcol'), may hold values from 0 to 1, as said below
Outputs:
- ancestor: float32 [4, 16, 32, 32768], P('prow', 'layer', None, 'pcol')
- lower: bfloat16 [16, 2048, 512], P('layer', 'prow')
- upper: bfloat16 [16, 256, 32768], P('layer', 'prow', 'pcol')
Inputs may be any that keep to these rules, and one draw needn't show every extreme that they name: `pivot_pattern`: each entry says whether that block of the pivot rows is structurally nonzero. `slab_pattern`: each entry says whether that block of the front rows is structurally nonzero.
All inputs are finite; a program needn't handle non-finite values.
Results may differ from a plain program's by a relative error of at most 0.014.
Values may be sent and summed in bfloat16 or wider, within the bound.
No kernel may reach another device: no remote copies, remote signals or barrier semaphores. Data moves between devices by JAX's collectives and lax.ppermute only.
A program may use at most 192 MiB of HBM per device.

v0:
```python
import jax
import jax.numpy as jnp
from jax import lax
from jax.sharding import PartitionSpec as P


def ring(value, axis, size, step):
    return lax.ppermute(value, axis, [(i, (i + step) % size) for i in range(size)])


def gather_relative(value, axis, size):
    from_prev = ring(value, axis, size, 1)
    from_next = ring(value, axis, size, -1)
    half = value.shape[1] // 2
    far_lo = ring(from_prev[:, :half], axis, size, 1)
    far_hi = ring(from_next[:, half:], axis, size, -1)
    far = jnp.concatenate([far_lo, far_hi], 1)
    return jnp.concatenate([value, from_next, far, from_prev], 1)


def grid_shift(value, axis, side, dy, dx):
    pairs = []
    for y in range(side):
        for x in range(side):
            pairs.append((y * side + x, (y + dy) % side * side + (x + dx) % side))
    return lax.ppermute(value, axis, pairs)


def ring_reduce(blocks, send):
    half = blocks.shape[1] // 2
    far = blocks[2].astype(jnp.bfloat16)
    fwd1 = send(far[:half], 1)
    bwd1 = send(far[half:], -1)
    next_block = blocks[1]
    prev_block = blocks[3]
    fwd2 = send(
        jnp.concatenate(
            [next_block[:half] + fwd1.astype(jnp.float32), next_block[half:]], 0
        ).astype(jnp.bfloat16),
        1,
    )
    bwd2 = send(
        jnp.concatenate(
            [prev_block[:half], prev_block[half:] + bwd1.astype(jnp.float32)], 0
        ).astype(jnp.bfloat16),
        -1,
    )
    return blocks[0] + fwd2.astype(jnp.float32) + bwd2.astype(jnp.float32)


def relative(value, own, axis):
    return jnp.stack(
        [lax.dynamic_index_in_dim(value, (own + j) % 4, axis, keepdims=False) for j in range(4)], 0
    )


def grid_reduce_scatter(left, right, axis):
    side = 4
    index = lax.axis_index(axis)
    gy = index // side
    gx = index % side
    rows, width = left.shape
    part = rows // (side * side)
    left = left.reshape(side, side, part, width)
    right = right.reshape(side, side, part, width)

    def along_x(v, step):
        return grid_shift(v, axis, side, 0, step)

    def along_y(v, step):
        return grid_shift(v, axis, side, step, 0)

    left = ring_reduce(relative(left, gx, 1), along_x)
    left = ring_reduce(relative(left, gy, 0), along_y)
    right = ring_reduce(relative(right, gy, 0), along_y)
    right = ring_reduce(relative(right, gx, 0), along_x)
    return jnp.concatenate([left, right], 1)


def on_device(front, pivots, inverses, slab_pattern, pivot_pattern):
    block_size = inverses.shape[-1]
    panel_width = 2 * block_size
    row_count = front.shape[1]
    col_count = front.shape[2]
    own_rows = pivots.shape[2]
    masked = (
        front[0].reshape(row_count // block_size, block_size, col_count // block_size, block_size)
        * slab_pattern[0].astype(jnp.bfloat16)[:, None, :, None]
    ).reshape(row_count, col_count)

    def mask_pivots(lo, hi):
        return (
            pivots[0, :, :, lo:hi].reshape(2, own_rows, (hi - lo) // block_size, block_size)
            * pivot_pattern[0, :, lo // block_size : hi // block_size].astype(jnp.bfloat16)[
                :, None, :, None
            ]
        ).reshape(2, own_rows, hi - lo)

    first_inverse = inverses[0, 0]
    second_inverse = inverses[0, 1]
    row_offset = lax.axis_index("prow") * own_rows
    pcol = lax.axis_index("pcol")
    n_prow = lax.axis_size("prow")
    n_pcol = lax.axis_size("pcol")
    assert n_prow == 4
    half = col_count * 11 // 16 // block_size * block_size
    first_cols = mask_pivots(0, half)
    gathered = lax.all_gather(first_cols, "prow", axis=1, tiled=True)
    later_cols, gathered = lax.optimization_barrier((mask_pivots(half, col_count), gathered))
    panel = jnp.roll(
        gather_relative(first_cols[:, :, :panel_width], "prow", n_prow), row_offset, axis=1
    )
    front_cols = masked[:, :panel_width]
    pivot_cols = panel[0]
    second_cols = panel[1]
    lower_pivot = jnp.dot(
        second_cols[:, :block_size], first_inverse, preferred_element_type=jnp.float32
    ).astype(jnp.bfloat16)
    lower_first = jnp.dot(
        front_cols[:, :block_size], first_inverse, preferred_element_type=jnp.float32
    ).astype(jnp.bfloat16)
    carried = (
        front_cols[:, block_size:].astype(jnp.float32)
        - jnp.dot(
            lower_first, pivot_cols[:, block_size:panel_width], preferred_element_type=jnp.float32
        )
    ).astype(jnp.bfloat16)
    lower_second = jnp.dot(carried, second_inverse, preferred_element_type=jnp.float32).astype(
        jnp.bfloat16
    )
    lower_panel = jnp.concatenate([lower_first, lower_second], 1)
    sent = lax.ppermute((lower_panel, lower_pivot), "pcol", [(0, i) for i in range(1, n_pcol)])
    on_root = pcol == 0
    lower_panel = jnp.where(on_root, lower_panel, sent[0])
    lower_pivot = jnp.where(on_root, lower_pivot, sent[1])
    folded = (
        lower_panel[:, :block_size].astype(jnp.float32)
        - jnp.dot(lower_panel[:, block_size:], lower_pivot, preferred_element_type=jnp.float32)
    ).astype(jnp.bfloat16)
    multipliers = jnp.concatenate([folded, lower_panel[:, block_size:]], 1)
    multipliers_rel = jnp.concatenate(
        [
            jnp.roll(folded, -row_offset, axis=1),
            jnp.roll(lower_panel[:, block_size:], -row_offset, axis=1),
        ],
        1,
    )
    col_index = pcol * col_count + jnp.arange(col_count, dtype=jnp.int32)
    retained = col_index >= panel_width
    schur_first = masked[:, :half].astype(jnp.float32) - jnp.dot(
        multipliers, gathered.reshape(2 * block_size, half), preferred_element_type=jnp.float32
    )
    schur_first = jnp.where(retained[None, :half], schur_first, jnp.zeros_like(schur_first))
    second_half = later_cols
    schur_first = schur_first.astype(jnp.bfloat16)
    summed_first = lax.psum_scatter(schur_first, "layer", scatter_dimension=0, tiled=True).astype(
        jnp.float32
    )
    gathered_rel = gather_relative(second_half, "prow", n_prow)
    own_pivot = lax.dynamic_slice_in_dim(lower_pivot, row_offset, own_rows, 0)
    upper_own = jnp.concatenate(
        [
            (
                first_cols[1].astype(jnp.float32)
                - jnp.dot(own_pivot, gathered[0], preferred_element_type=jnp.float32)
            ).astype(jnp.bfloat16),
            (
                later_cols[1].astype(jnp.float32)
                - jnp.dot(
                    jnp.roll(own_pivot, -row_offset, axis=1),
                    gathered_rel[0],
                    preferred_element_type=jnp.float32,
                )
            ).astype(jnp.bfloat16),
        ],
        1,
    )
    split = (col_count - half) // 2
    stacked_rel = gathered_rel.reshape(2 * block_size, col_count - half)
    schur_halves = []
    for start in (0, split):
        cols = slice(half + start, half + start + split)
        schur_half = masked[:, cols].astype(jnp.float32) - jnp.dot(
            multipliers_rel,
            stacked_rel[:, start : start + split],
            preferred_element_type=jnp.float32,
        )
        schur_halves.append(jnp.where(retained[None, cols], schur_half, jnp.zeros_like(schur_half)))
    summed = jnp.concatenate([summed_first, grid_reduce_scatter(*schur_halves, "layer")], 1)
    ancestor = summed.reshape(1, 1, summed.shape[0], col_count)
    return (ancestor, lower_panel[None], upper_own[None])


def solution(mesh):
    placed = (
        P("layer", "prow", "pcol"),
        P("layer", None, "prow", "pcol"),
        P("layer", None, None, None),
        P("layer", "prow", "pcol"),
        P("layer", None, "pcol"),
    )
    return jax.shard_map(
        on_device,
        mesh=mesh,
        in_specs=placed,
        out_specs=(
            P("prow", "layer", None, "pcol"),
            P("layer", "prow", None),
            P("layer", "prow", "pcol"),
        ),
        check_vma=False,
    )
```

profile of v0, /device:TPU:1, one launch (start us, length us, event | category | flops | bytes accessed | tf_op | source)
XLA Modules:
  0.0 258.3 jit_solution(1569205453357182786)
XLA Ops:
  7.2 0.7 convert.70
  8.0 3.6 %bitcast_multiply_fusion.1 = bf16[2,64,11264]{2,1,0:T(8,128)(2,1)} fusion(bf16[2,11264]{1,0:T(2,128)(2,1)S(1)} %bitcast.177, bf16[1,2,64,16384]{3,2,1,0:T(8,128)(2,1)} %param.8), kind=kLoop, calls=%fused_computation.10 | loop fusion | flops 1441792 | bytes 5812224 | tf_op jit(solution)/shard_map/mul | solution.py:93
  11.7 1.6 fusion.61
  13.3 4.6 %collective-permute-start = (bf16[2,64,512]{2,1,0:T(8,128)(2,1)S(1)}, bf16[2,64,512]{2,1,0:T(8,128)(2,1)S(1)}, u32[]{:S(2)}, u32[]{:S(2)}) collective-permute-start(bf16[2,64,512]{2,1,0:T(8,128)(2,1)S(1)} %get-tuple-element.20), channel_id=1, source_target_pairs={{0,6},{2,0},{4,2},{6,4},{1,7},{3,1},{5,3},{7,5},{8,14},{10,8},{12,... | collective-permute-start | bytes 393224 | tf_op jit(solution)/shard_map/ppermute | solution.py:8
  18.1 3.0 %reshape_squeeze.14 = bf16[2,64,44,256]{3,2,1,0:T(8,128)(2,1)} reshape(bf16[1,2,64,11264]{3,2,1,0:T(8,128)(2,1)S(1)} %slice-done) | data formatting | bytes 5767168 | tf_op jit(solution)/shard_map/reshape;squeeze | solution.py:93
  21.1 1.7 fusion.6
  22.7 1.6 copy.19
  24.4 2.7 %mul.48 = bf16[2,256,64,256]{3,2,1,0:T(8,128)(2,1)S(1)} broadcast(bf16[2,64]{1,0:T(2,128)(2,1)S(1)} %convert_bitcast_fusion), dimensions={0,2} | broadcast | bytes 16777472 | tf_op jit(solution)/shard_map/mul | solution.py:87
  27.2 12.4 %copy.16 = bf16[64,8,64,256]{3,1,2,0:T(8,128)(2,1)} copy(bf16[64,8,64,256]{3,2,1,0:T(8,128)(2,1)S(1)} %bitcast.163) | data formatting | bytes 33554432
  39.7 2.5 bitcast_multiply_fusion.2
  42.2 12.2 %bitcast_multiply_fusion = bf16[512,16384]{1,0:T(8,128)(2,1)S(1)} fusion(bf16[512,16384]{1,0:T(8,128)(2,1)} %bitcast.162, bf16[1,512,16384]{2,1,0:T(8,128)(2,1)} %param.7), kind=kLoop, calls=%fused_computation.1 | loop fusion | flops 8388608 | bytes 50331648 | tf_op jit(solution)/shard_map/mul | solution.py:87
  54.4 5.8 %copy-done = bf16[512,16384]{1,0:T(8,128)(2,1)} copy-done((bf16[512,16384]{1,0:T(8,128)(2,1)}, bf16[512,16384]{1,0:T(8,128)(2,1)S(1)}, u32[]{:S(2)}) %copy-start) | copy-done | bytes 16777240
  60.6 2.7 %collective-permute-start.3 = (bf16[2,32,512]{2,1,0:T(8,128)(2,1)S(1)}, bf16[2,32,512]{2,1,0:T(8,128)(2,1)S(1)}, u32[]{:S(2)}, u32[]{:S(2)}) collective-permute-start(bf16[2,32,512]{2,1,0:T(8,128)(2,1)S(1)} %slice.338), channel_id=1, source_target_pairs={{0,6},{2,0},{4,2},{6,4},{1,7},{3,1},{5,3},{7,5},{8,14},{10,8},{12,... | collective-permute-start | bytes 196616 | tf_op jit(solution)/shard_map/ppermute | solution.py:8
  63.4 3.6 %collective-permute-done.2 = bf16[2,32,512]{2,1,0:T(8,128)(2,1)S(1)} collective-permute-done((bf16[2,32,512]{2,1,0:T(8,128)(2,1)S(1)}, bf16[2,32,512]{2,1,0:T(8,128)(2,1)S(1)}, u32[]{:S(2)}, u32[]{:S(2)}) %collective-permute-start.2) | collective-permute-done | bytes 65568 | tf_op jit(solution)/shard_map/ppermute | solution.py:8
  67.0 0.9 constant_dynamic-update-slice_fusion.4
  68.0 0.7 dynamic-slice_bitcast_fusion.4
  68.9 1.3 collective-permute-start.5
  70.2 1.5 convolution_convert_fusion
  71.8 1.3 collective-permute-start.4
  73.7 0.9 broadcast_select_fusion.1
  74.7 0.6 copy-done.7
  75.3 1.5 collective-permute-done.4
  76.8 1.2 broadcast_select_fusion
  78.0 0.7 slice.341
  78.7 1.0 copy.12
  79.7 1.9 subtract_convert_fusion
  81.6 44.8 %all-gather.2.cloned.1.call-done = bf16[2,256,11264]{2,1,0:T(8,128)(2,1)} async-done(((bf16[2,64,11264]{2,1,0:T(8,128)(2,1)}), bf16[2,256,11264]{2,1,0:T(8,128)(2,1)}) %all-gather.2.cloned.1.call-update) | async-done | bytes 11534352 | tf_op jit(solution)/shard_map/all_gather | solution.py:108
  126.4 0.9 collective-permute-start.6
  127.8 13.9 %select_convert_fusion = bf16[512,11264]{1,0:T(8,128)(2,1)} fusion(bf16[512,11264]{1,0:T(8,128)(2,1)} %bitcast.176, bf16[512,16384]{1,0:T(8,128)(2,1)} %copy-done, pred[11264]{0:T(1024)(128)(4,1)S(1)} %slice-done.1, bf16[512,256]{0,1:T(8,128)(2,1)} %slice.341, bf16[512,256]{0,1:T(8,128)(2,1)} %subtract_convert_fusion), kind=kOutput, calls=%fused_computation | convolution fusion | flops 5929697280 | bytes 35138560 | tf_op jit(solution)/shard_map/dot_general | solution.py:150
  141.7 0.9 copy-done.3
  142.6 1.4 fusion.25
  144.0 1.4 constant_dynamic-update-slice_fusion.14
  145.4 12.5 %collective-permute-done.7 = bf16[2,64,5120]{2,1,0:T(8,128)(2,1)} collective-permute-done((bf16[2,64,5120]{2,1,0:T(8,128)(2,1)}, bf16[2,64,5120]{2,1,0:T(8,128)(2,1)}, u32[]{:S(2)}, u32[]{:S(2)}) %collective-permute-start.7) | collective-permute-done | bytes 1310752 | tf_op jit(solution)/shard_map/ppermute | solution.py:8
  157.9 1.1 slice.345
  159.2 3.9 %fusion = bf16[64,11264]{1,0:T(8,128)(2,1)S(1)} fusion(f32[64,11264]{1,0:T(8,128)S(1)} %bitcast.165, bf16[64,256]{1,0:T(8,128)(2,1)S(1)} %constant_dynamic-slice_fusion, bf16[2,256,11264]{2,1,0:T(8,128)(2,1)} %all-gather.2.cloned.1.call-done), kind=kOutput, calls=%fused_computation.3 | convolution fusion | flops 370540544 | bytes 10125312 | tf_op jit(solution)/shard_map/dot_general | solution.py:165
  163.1 1.1 slice.346
  164.2 2.7 %collective-permute-start.9 = (bf16[2,32,5120]{2,1,0:T(8,128)(2,1)S(1)}, bf16[2,32,5120]{2,1,0:T(8,128)(2,1)S(1)}, u32[]{:S(2)}, u32[]{:S(2)}) collective-permute-start(bf16[2,32,5120]{2,1,0:T(8,128)(2,1)S(1)} %slice.346), channel_id=1, source_target_pairs={{0,6},{2,0},{4,2},{6,4},{1,7},{3,1},{5,3},{7,5},{8,14},{10,8},{12,... | collective-permute-start | bytes 1966088 | tf_op jit(solution)/shard_map/ppermute | solution.py:8
  166.9 1.5 constant_dynamic-update-slice_fusion.13
  168.5 6.2 %collective-permute-done.8 = bf16[2,32,5120]{2,1,0:T(8,128)(2,1)S(1)} collective-permute-done((bf16[2,32,5120]{2,1,0:T(8,128)(2,1)S(1)}, bf16[2,32,5120]{2,1,0:T(8,128)(2,1)S(1)}, u32[]{:S(2)}, u32[]{:S(2)}) %collective-permute-start.8) | collective-permute-done | bytes 655392 | tf_op jit(solution)/shard_map/ppermute | solution.py:8
  174.7 4.1 %collective-permute-done.9 = bf16[2,32,5120]{2,1,0:T(8,128)(2,1)S(1)} collective-permute-done((bf16[2,32,5120]{2,1,0:T(8,128)(2,1)S(1)}, bf16[2,32,5120]{2,1,0:T(8,128)(2,1)S(1)}, u32[]{:S(2)}, u32[]{:S(2)}) %collective-permute-start.9) | collective-permute-done | bytes 655392 | tf_op jit(solution)/shard_map/ppermute | solution.py:8
  178.8 1.5 constant_dynamic-update-slice_fusion.10
  180.4 3.6 %subtract_select_fusion.1 = f32[512,2560]{1,0:T(8,128)S(1)} fusion(bf16[512,5120]{1,0:T(8,128)(2,1)S(1)} %bitcast.174, bf16[512,16384]{1,0:T(8,128)(2,1)} %copy-done, pred[2560]{0:T(1024)(128)(4,1)S(1)} %copy-done.10, bf16[512,256]{0,1:T(8,128)(2,1)S(1)} %get-tuple-element.42, bf16[512,256]{0,1:T(8,128)(2,1)S(1)} %get-tuple-element.43), kind=kOutput, calls=%fused_computation.9 | convolution fusion | flops 1347158016 | bytes 11013120 | tf_op jit(solution)/shard_map/dot_general | solution.py:183
  184.1 1.8 collective-permute-start.10
  185.9 1.1 collective-permute-start.12
  187.1 3.5 %subtract_select_fusion = f32[512,2560]{1,0:T(8,128)S(1)} fusion(bf16[512,5120]{1,0:T(8,128)(2,1)S(1)} %bitcast.175, bf16[512,16384]{1,0:T(8,128)(2,1)} %copy-done, pred[2560]{0:T(1024)(128)(4,1)S(1)} %copy-done.9, bf16[512,256]{0,1:T(8,128)(2,1)S(1)} %get-tuple-element.42, bf16[512,256]{0,1:T(8,128)(2,1)S(1)} %get-tuple-element.43), kind=kOutput, calls=%fused_computation.8 | convolution fusion | flops 1347158016 | bytes 11013120 | tf_op jit(solution)/shard_map/dot_general | solution.py:183
  190.7 1.6 collective-permute-start.18
  192.3 1.2 collective-permute-start.20
  193.5 0.7 fusion.1
  194.5 1.5 maximum_bitcast_fusion.1
  196.0 5.0 %collective-permute-done.10 = bf16[2,32,2560]{2,1,0:T(8,128)(2,1)S(1)} collective-permute-done((bf16[2,32,2560]{2,1,0:T(8,128)(2,1)S(1)}, bf16[2,32,2560]{2,1,0:T(8,128)(2,1)S(1)}, u32[]{:S(2)}, u32[]{:S(2)}) %collective-permute-start.10) | collective-permute-done | bytes 327712 | tf_op jit(solution)/shard_map/ppermute | solution.py:26
  201.1 1.0 collective-permute-start.11
  202.3 2.0 collective-permute-start.13
  204.3 2.4 collective-permute-done.18
  207.1 2.7 %collective-permute-start.21 = (bf16[4,32,2560]{2,1,0:T(8,128)(2,1)S(1)}, bf16[4,32,2560]{2,1,0:T(8,128)(2,1)S(1)}, u32[]{:S(2)}, u32[]{:S(2)}) collective-permute-start(bf16[4,32,2560]{2,1,0:T(8,128)(2,1)S(1)} %pad_maximum_fusion.3), channel_id=1, source_target_pairs={{0,96},{8,104},{16,112},{24,120},{32,0},{40,8},{48,16},{56,24},{64... | collective-permute-start | bytes 1966088 | tf_op jit(solution)/shard_map/ppermute | solution.py:26
  209.8 15.2 %collective-permute-done.11 = bf16[4,32,2560]{2,1,0:T(8,128)(2,1)S(1)} collective-permute-done((bf16[4,32,2560]{2,1,0:T(8,128)(2,1)S(1)}, bf16[4,32,2560]{2,1,0:T(8,128)(2,1)S(1)}, u32[]{:S(2)}, u32[]{:S(2)}) %collective-permute-start.11) | collective-permute-done | bytes 655392 | tf_op jit(solution)/shard_map/ppermute | solution.py:26
  225.6 2.4 collective-permute-start.16
  228.8 2.4 collective-permute-start.24
  231.4 3.3 %collective-permute-start.17 = (bf16[32,2560]{1,0:T(8,128)(2,1)S(1)}, bf16[32,2560]{1,0:T(8,128)(2,1)S(1)}, u32[]{:S(2)}, u32[]{:S(2)}) collective-permute-start(bf16[32,2560]{1,0:T(8,128)(2,1)S(1)} %pad_maximum_fusion.11), channel_id=1, source_target_pairs={{0,96},{8,104},{16,112},{24,120},{32,0},{40,8},{48,16},{56,24},{64... | collective-permute-start | bytes 491528 | tf_op jit(solution)/shard_map/ppermute | solution.py:26
  235.3 2.6 %collective-permute-start.25 = (bf16[32,2560]{1,0:T(8,128)(2,1)S(1)}, bf16[32,2560]{1,0:T(8,128)(2,1)S(1)}, u32[]{:S(2)}, u32[]{:S(2)}) collective-permute-start(bf16[32,2560]{1,0:T(8,128)(2,1)S(1)} %pad_maximum_fusion.13), channel_id=1, source_target_pairs={{0,24},{8,0},{16,8},{24,16},{32,56},{40,32},{48,40},{56,48},{64,88... | collective-permute-start | bytes 491528 | tf_op jit(solution)/shard_map/ppermute | solution.py:26
  237.9 2.6 %collective-permute-done.15 = bf16[32,2560]{1,0:T(8,128)(2,1)S(1)} collective-permute-done((bf16[32,2560]{1,0:T(8,128)(2,1)S(1)}, bf16[32,2560]{1,0:T(8,128)(2,1)S(1)}, u32[]{:S(2)}, u32[]{:S(2)}) %collective-permute-start.15) | collective-permute-done | bytes 163872 | tf_op jit(solution)/shard_map/ppermute | solution.py:26
  240.9 3.8 %collective-permute-done.23 = bf16[32,2560]{1,0:T(8,128)(2,1)S(1)} collective-permute-done((bf16[32,2560]{1,0:T(8,128)(2,1)S(1)}, bf16[32,2560]{1,0:T(8,128)(2,1)S(1)}, u32[]{:S(2)}, u32[]{:S(2)}) %collective-permute-start.23) | collective-permute-done | bytes 163872 | tf_op jit(solution)/shard_map/ppermute | solution.py:26
  244.7 4.1 %reduce-scatter.2.cloned.1.call-done = bf16[32,11264]{1,0:T(8,128)(2,1)} async-done(((bf16[512,11264]{1,0:T(8,128)(2,1)}), bf16[32,11264]{1,0:T(8,128)(2,1)}) %reduce-scatter.2.cloned.1.call-update) | async-done | bytes 720912 | tf_op jit(solution)/shard_map/reduce_scatter | solution.py:156
  248.8 1.2 convert_element_type.165
  250.0 1.5 maximum_bitcast_fusion
  (111 shorter events, 6.0 us)
Async XLA Ops:
  7.2 119.2 %all-gather.2.cloned.1.call-start = ((), (), s32[]{:S(2)}) async-start(), calls=%async_computation.1 | async-start | bytes 14417920 | tf_op jit(solution)/shard_map/all_gather | solution.py:108
  11.7 237.2 %reduce-scatter.2.cloned.1.call-start = ((), (), s32[]{:S(2)}) async-start(), calls=%async_computation.2 | async-start | bytes 12255232 | tf_op jit(solution)/shard_map/reduce_scatter | solution.py:156
  13.3 4.8 %slice-start = ((bf16[1,2,64,16384]{3,2,1,0:T(8,128)(2,1)}), bf16[1,2,64,11264]{3,2,1,0:T(8,128)(2,1)S(1)}, s32[]{:S(2)}) async-start(bf16[1,2,64,16384]{3,2,1,0:T(8,128)(2,1)} %param.8), calls=%async_computation.3 | async-start | bytes 5767168 | tf_op jit(solution)/shard_map/slice | solution.py:93
  13.3 47.3 %collective-permute-start = (bf16[2,64,512]{2,1,0:T(8,128)(2,1)S(1)}, bf16[2,64,512]{2,1,0:T(8,128)(2,1)S(1)}, u32[]{:S(2)}, u32[]{:S(2)}) collective-permute-start(bf16[2,64,512]{2,1,0:T(8,128)(2,1)S(1)} %get-tuple-element.20), channel_id=1, source_target_pairs={{0,6},{2,0},{4,2},{6,4},{1,7},{3,1},{5,3},{7,5},{8,14},{10,8},{12,... | collective-permute-start | bytes 393224 | tf_op jit(solution)/shard_map/ppermute | solution.py:8
  17.9 42.6 %collective-permute-start.1 = (bf16[2,64,512]{2,1,0:T(8,128)(2,1)S(1)}, bf16[2,64,512]{2,1,0:T(8,128)(2,1)S(1)}, u32[]{:S(2)}, u32[]{:S(2)}) collective-permute-start(bf16[2,64,512]{2,1,0:T(8,128)(2,1)S(1)} %get-tuple-element.20), channel_id=1, source_target_pairs={{0,2},{2,4},{4,6},{6,0},{1,3},{3,5},{5,7},{7,1},{8,10},{10,12},{12... | collective-permute-start | bytes 393224 | tf_op jit(solution)/shard_map/ppermute | solution.py:8
  22.7 1.7 copy-start.11
  39.6 33.5 %copy-start.8 = (pred[16384]{0:T(1024)(128)(4,1)}, pred[16384]{0:T(1024)(128)(4,1)S(1)}, u32[]{:S(2)}) copy-start(pred[16384]{0:T(1024)(128)(4,1)S(1)} %add_compare_fusion) | copy-start | bytes 49156
  42.2 18.0 %copy-start.6 = (bf16[1,2,256,256]{3,2,1,0:T(8,128)(2,1)S(1)}, bf16[1,2,256,256]{3,2,1,0:T(8,128)(2,1)}, u32[]{:S(2)}) copy-start(bf16[1,2,256,256]{3,2,1,0:T(8,128)(2,1)} %param.9) | copy-start | bytes 786436
  42.2 21.2 %copy-start.5 = (bf16[2,512,512]{2,1,0:T(8,128)(2,1)S(1)}, bf16[2,512,512]{2,1,0:T(8,128)(2,1)}, u32[]{:S(2)}) copy-start(bf16[2,512,512]{2,1,0:T(8,128)(2,1)} %get-tuple-element.21) | copy-start | bytes 3145732
  54.4 5.8 %copy-start = (bf16[512,16384]{1,0:T(8,128)(2,1)}, bf16[512,16384]{1,0:T(8,128)(2,1)S(1)}, u32[]{:S(2)}) copy-start(bf16[512,16384]{1,0:T(8,128)(2,1)S(1)} %bitcast_multiply_fusion) | copy-start | bytes 50331652
  60.5 14.2 %copy-start.2 = (bf16[512,256]{0,1:T(8,128)(2,1)}, bf16[512,256]{0,1:T(8,128)(2,1)S(1)}, u32[]{:S(2)}) copy-start(bf16[512,256]{0,1:T(8,128)(2,1)S(1)} %convolution_convert_fusion.1) | copy-start | bytes 786436
  60.5 6.4 %collective-permute-start.2 = (bf16[2,32,512]{2,1,0:T(8,128)(2,1)S(1)}, bf16[2,32,512]{2,1,0:T(8,128)(2,1)S(1)}, u32[]{:S(2)}, u32[]{:S(2)}) collective-permute-start(bf16[2,32,512]{2,1,0:T(8,128)(2,1)S(1)} %slice.337), channel_id=1, source_target_pairs={{0,2},{2,4},{4,6},{6,0},{1,3},{3,5},{5,7},{7,1},{8,10},{10,12},{12... | collective-permute-start | bytes 196616 | tf_op jit(solution)/shard_map/ppermute | solution.py:8
  60.6 6.3 %collective-permute-start.3 = (bf16[2,32,512]{2,1,0:T(8,128)(2,1)S(1)}, bf16[2,32,512]{2,1,0:T(8,128)(2,1)S(1)}, u32[]{:S(2)}, u32[]{:S(2)}) collective-permute-start(bf16[2,32,512]{2,1,0:T(8,128)(2,1)S(1)} %slice.338), channel_id=1, source_target_pairs={{0,6},{2,0},{4,2},{6,4},{1,7},{3,1},{5,3},{7,5},{8,14},{10,8},{12,... | collective-permute-start | bytes 196616 | tf_op jit(solution)/shard_map/ppermute | solution.py:8
  68.9 4.8 %collective-permute-start.5 = (bf16[256,256]{1,0:T(8,128)(2,1)S(1)}, bf16[256,256]{1,0:T(8,128)(2,1)}, u32[]{:S(2)}, u32[]{:S(2)}) collective-permute-start(bf16[256,256]{1,0:T(8,128)(2,1)S(1)} %convolution_convert_fusion.2), channel_id=1, source_target_pairs={{0,1},{2,3},{4,5},{6,7},{8,9},{10,11},{12,13},{14,15},{16,17},{18,... | collective-permute-start | bytes 393224 | tf_op jit(solution)/shard_map/ppermute | solution.py:132
  71.7 2.9 %copy-start.4 = (bf16[512,256]{0,1:T(8,128)(2,1)}, bf16[512,256]{0,1:T(8,128)(2,1)S(1)}, u32[]{:S(2)}) copy-start(bf16[512,256]{0,1:T(8,128)(2,1)S(1)} %convolution_convert_fusion) | copy-start | bytes 786436
  71.8 5.0 %collective-permute-start.4 = (bf16[512,512]{0,1:T(8,128)(2,1)S(1)}, bf16[512,512]{0,1:T(8,128)(2,1)S(1)}, u32[]{:S(2)}, u32[]{:S(2)}) collective-permute-start(bf16[512,512]{0,1:T(8,128)(2,1)S(1)} %pad_maximum_fusion.6), channel_id=1, source_target_pairs={{0,1},{2,3},{4,5},{6,7},{8,9},{10,11},{12,13},{14,15},{16,17},{18,... | collective-permute-start | bytes 1572872 | tf_op jit(solution)/shard_map/ppermute | solution.py:132
  73.7 54.1 %slice-start.1 = ((pred[16384]{0:T(1024)(128)(4,1)}), pred[11264]{0:T(1024)(128)(4,1)S(1)}, s32[]{:S(2)}) async-start(pred[16384]{0:T(1024)(128)(4,1)} %copy-done.8), calls=%async_computation.4 | async-start | bytes 22528 | tf_op jit(solution)/shard_map/slice | solution.py:153
  74.6 0.7 copy-start.7
  126.4 36.7 %collective-permute-start.6 = (bf16[2,64,5120]{2,1,0:T(8,128)(2,1)}, bf16[2,64,5120]{2,1,0:T(8,128)(2,1)}, u32[]{:S(2)}, u32[]{:S(2)}) collective-permute-start(bf16[2,64,5120]{2,1,0:T(8,128)(2,1)} %bitcast_multiply_fusion.2), channel_id=1, source_target_pairs={{0,6},{2,0},{4,2},{6,4},{1,7},{3,1},{5,3},{7,5},{8,14},{10,8},{12,... | collective-permute-start | bytes 3932168 | tf_op jit(solution)/shard_map/ppermute | solution.py:8
  127.2 30.7 %collective-permute-start.7 = (bf16[2,64,5120]{2,1,0:T(8,128)(2,1)}, bf16[2,64,5120]{2,1,0:T(8,128)(2,1)}, u32[]{:S(2)}, u32[]{:S(2)}) collective-permute-start(bf16[2,64,5120]{2,1,0:T(8,128)(2,1)} %bitcast_multiply_fusion.2), channel_id=1, source_target_pairs={{0,2},{2,4},{4,6},{6,0},{1,3},{3,5},{5,7},{7,1},{8,10},{10,12},{12... | collective-permute-start | bytes 3932168 | tf_op jit(solution)/shard_map/ppermute | solution.py:8
  141.7 0.9 copy-start.3
  159.1 15.6 %collective-permute-start.8 = (bf16[2,32,5120]{2,1,0:T(8,128)(2,1)S(1)}, bf16[2,32,5120]{2,1,0:T(8,128)(2,1)S(1)}, u32[]{:S(2)}, u32[]{:S(2)}) collective-permute-start(bf16[2,32,5120]{2,1,0:T(8,128)(2,1)S(1)} %slice.345), channel_id=1, source_target_pairs={{0,2},{2,4},{4,6},{6,0},{1,3},{3,5},{5,7},{7,1},{8,10},{10,12},{12... | collective-permute-start | bytes 1966088 | tf_op jit(solution)/shard_map/ppermute | solution.py:8
  164.2 14.5 %collective-permute-start.9 = (bf16[2,32,5120]{2,1,0:T(8,128)(2,1)S(1)}, bf16[2,32,5120]{2,1,0:T(8,128)(2,1)S(1)}, u32[]{:S(2)}, u32[]{:S(2)}) collective-permute-start(bf16[2,32,5120]{2,1,0:T(8,128)(2,1)S(1)} %slice.346), channel_id=1, source_target_pairs={{0,6},{2,0},{4,2},{6,4},{1,7},{3,1},{5,3},{7,5},{8,14},{10,8},{12,... | collective-permute-start | bytes 1966088 | tf_op jit(solution)/shard_map/ppermute | solution.py:8
  168.5 11.9 %copy-start.10 = (pred[2560]{0:T(1024)(128)(4,1)S(1)}, pred[2560]{0:T(1024)(128)(4,1)}, u32[]{:S(2)}) copy-start(pred[2560]{0:T(1024)(128)(4,1)} %get-tuple-element.40) | copy-start | bytes 7684
  180.4 6.7 %copy-start.9 = (pred[2560]{0:T(1024)(128)(4,1)S(1)}, pred[2560]{0:T(1024)(128)(4,1)}, u32[]{:S(2)}) copy-start(pred[2560]{0:T(1024)(128)(4,1)} %get-tuple-element.41) | copy-start | bytes 7684
  184.1 16.9 %collective-permute-start.10 = (bf16[2,32,2560]{2,1,0:T(8,128)(2,1)S(1)}, bf16[2,32,2560]{2,1,0:T(8,128)(2,1)S(1)}, u32[]{:S(2)}, u32[]{:S(2)}) collective-permute-start(bf16[2,32,2560]{2,1,0:T(8,128)(2,1)S(1)} %get-tuple-element.32), channel_id=1, source_target_pairs={{0,8},{8,16},{16,24},{24,0},{32,40},{40,48},{48,56},{56,32},{64,72... | collective-permute-start | bytes 983048 | tf_op jit(solution)/shard_map/ppermute | solution.py:26
  185.9 16.2 %collective-permute-start.12 = (bf16[2,32,2560]{2,1,0:T(8,128)(2,1)S(1)}, bf16[2,32,2560]{2,1,0:T(8,128)(2,1)S(1)}, u32[]{:S(2)}, u32[]{:S(2)}) collective-permute-start(bf16[2,32,2560]{2,1,0:T(8,128)(2,1)S(1)} %get-tuple-element.33), channel_id=1, source_target_pairs={{0,24},{8,0},{16,8},{24,16},{32,56},{40,32},{48,40},{56,48},{64,88... | collective-permute-start | bytes 983048 | tf_op jit(solution)/shard_map/ppermute | solution.py:26
  187.1 6.5 %copy-start.1 = (bf16[2,64,5120]{2,1,0:T(8,128)(2,1)S(1)}, bf16[2,64,5120]{2,1,0:T(8,128)(2,1)}, u32[]{:S(2)}) copy-start(bf16[2,64,5120]{2,1,0:T(8,128)(2,1)} %bitcast_multiply_fusion.2) | copy-start | bytes 3932164
  190.7 16.0 %collective-permute-start.18 = (bf16[2,32,2560]{2,1,0:T(8,128)(2,1)S(1)}, bf16[2,32,2560]{2,1,0:T(8,128)(2,1)S(1)}, u32[]{:S(2)}, u32[]{:S(2)}) collective-permute-start(bf16[2,32,2560]{2,1,0:T(8,128)(2,1)S(1)} %get-tuple-element.34), channel_id=1, source_target_pairs={{0,32},{8,40},{16,48},{24,56},{32,64},{40,72},{48,80},{56,88},{64,... | collective-permute-start | bytes 983048 | tf_op jit(solution)/shard_map/ppermute | solution.py:26
  192.3 14.4 %collective-permute-start.20 = (bf16[2,32,2560]{2,1,0:T(8,128)(2,1)S(1)}, bf16[2,32,2560]{2,1,0:T(8,128)(2,1)S(1)}, u32[]{:S(2)}, u32[]{:S(2)}) collective-permute-start(bf16[2,32,2560]{2,1,0:T(8,128)(2,1)S(1)} %get-tuple-element.35), channel_id=1, source_target_pairs={{0,96},{8,104},{16,112},{24,120},{32,0},{40,8},{48,16},{56,24},{64... | collective-permute-start | bytes 983048 | tf_op jit(solution)/shard_map/ppermute | solution.py:26
  201.1 23.9 %collective-permute-start.11 = (bf16[4,32,2560]{2,1,0:T(8,128)(2,1)S(1)}, bf16[4,32,2560]{2,1,0:T(8,128)(2,1)S(1)}, u32[]{:S(2)}, u32[]{:S(2)}) collective-permute-start(bf16[4,32,2560]{2,1,0:T(8,128)(2,1)S(1)} %pad_maximum_fusion), channel_id=1, source_target_pairs={{0,8},{8,16},{16,24},{24,0},{32,40},{40,48},{48,56},{56,32},{64,72... | collective-permute-start | bytes 1966088 | tf_op jit(solution)/shard_map/ppermute | solution.py:26
  202.3 22.8 %collective-permute-start.13 = (bf16[4,32,2560]{2,1,0:T(8,128)(2,1)S(1)}, bf16[4,32,2560]{2,1,0:T(8,128)(2,1)S(1)}, u32[]{:S(2)}, u32[]{:S(2)}) collective-permute-start(bf16[4,32,2560]{2,1,0:T(8,128)(2,1)S(1)} %pad_maximum_fusion.1), channel_id=1, source_target_pairs={{0,24},{8,0},{16,8},{24,16},{32,56},{40,32},{48,40},{56,48},{64,88... | collective-permute-start | bytes 1966088 | tf_op jit(solution)/shard_map/ppermute | solution.py:26
  206.9 21.1 %collective-permute-start.19 = (bf16[4,32,2560]{2,1,0:T(8,128)(2,1)S(1)}, bf16[4,32,2560]{2,1,0:T(8,128)(2,1)S(1)}, u32[]{:S(2)}, u32[]{:S(2)}) collective-permute-start(bf16[4,32,2560]{2,1,0:T(8,128)(2,1)S(1)} %pad_maximum_fusion.2), channel_id=1, source_target_pairs={{0,32},{8,40},{16,48},{24,56},{32,64},{40,72},{48,80},{56,88},{64,... | collective-permute-start | bytes 1966088 | tf_op jit(solution)/shard_map/ppermute | solution.py:26
  207.1 21.0 %collective-permute-start.21 = (bf16[4,32,2560]{2,1,0:T(8,128)(2,1)S(1)}, bf16[4,32,2560]{2,1,0:T(8,128)(2,1)S(1)}, u32[]{:S(2)}, u32[]{:S(2)}) collective-permute-start(bf16[4,32,2560]{2,1,0:T(8,128)(2,1)S(1)} %pad_maximum_fusion.3), channel_id=1, source_target_pairs={{0,96},{8,104},{16,112},{24,120},{32,0},{40,8},{48,16},{56,24},{64... | collective-permute-start | bytes 1966088 | tf_op jit(solution)/shard_map/ppermute | solution.py:26
  225.3 5.9 %collective-permute-start.14 = (bf16[16,2560]{1,0:T(8,128)(2,1)S(1)}, bf16[16,2560]{1,0:T(8,128)(2,1)S(1)}, u32[]{:S(2)}, u32[]{:S(2)}) collective-permute-start(bf16[16,2560]{1,0:T(8,128)(2,1)S(1)} %get-tuple-element.36), channel_id=1, source_target_pairs={{0,32},{8,40},{16,48},{24,56},{32,64},{40,72},{48,80},{56,88},{64,... | collective-permute-start | bytes 245768 | tf_op jit(solution)/shard_map/ppermute | solution.py:26
  225.6 5.6 %collective-permute-start.16 = (bf16[16,2560]{1,0:T(8,128)(2,1)S(1)}, bf16[16,2560]{1,0:T(8,128)(2,1)S(1)}, u32[]{:S(2)}, u32[]{:S(2)}) collective-permute-start(bf16[16,2560]{1,0:T(8,128)(2,1)S(1)} %get-tuple-element.37), channel_id=1, source_target_pairs={{0,96},{8,104},{16,112},{24,120},{32,0},{40,8},{48,16},{56,24},{64... | collective-permute-start | bytes 245768 | tf_op jit(solution)/shard_map/ppermute | solution.py:26
  228.5 6.6 %collective-permute-start.22 = (bf16[16,2560]{1,0:T(8,128)(2,1)S(1)}, bf16[16,2560]{1,0:T(8,128)(2,1)S(1)}, u32[]{:S(2)}, u32[]{:S(2)}) collective-permute-start(bf16[16,2560]{1,0:T(8,128)(2,1)S(1)} %get-tuple-element.38), channel_id=1, source_target_pairs={{0,8},{8,16},{16,24},{24,0},{32,40},{40,48},{48,56},{56,32},{64,72... | collective-permute-start | bytes 245768 | tf_op jit(solution)/shard_map/ppermute | solution.py:26
  228.8 6.3 %collective-permute-start.24 = (bf16[16,2560]{1,0:T(8,128)(2,1)S(1)}, bf16[16,2560]{1,0:T(8,128)(2,1)S(1)}, u32[]{:S(2)}, u32[]{:S(2)}) collective-permute-start(bf16[16,2560]{1,0:T(8,128)(2,1)S(1)} %get-tuple-element.39), channel_id=1, source_target_pairs={{0,24},{8,0},{16,8},{24,16},{32,56},{40,32},{48,40},{56,48},{64,88... | collective-permute-start | bytes 245768 | tf_op jit(solution)/shard_map/ppermute | solution.py:26
  231.3 9.3 %collective-permute-start.15 = (bf16[32,2560]{1,0:T(8,128)(2,1)S(1)}, bf16[32,2560]{1,0:T(8,128)(2,1)S(1)}, u32[]{:S(2)}, u32[]{:S(2)}) collective-permute-start(bf16[32,2560]{1,0:T(8,128)(2,1)S(1)} %pad_maximum_fusion.10), channel_id=1, source_target_pairs={{0,32},{8,40},{16,48},{24,56},{32,64},{40,72},{48,80},{56,88},{64,... | collective-permute-start | bytes 491528 | tf_op jit(solution)/shard_map/ppermute | solution.py:26
  231.4 9.5 %collective-permute-start.17 = (bf16[32,2560]{1,0:T(8,128)(2,1)S(1)}, bf16[32,2560]{1,0:T(8,128)(2,1)S(1)}, u32[]{:S(2)}, u32[]{:S(2)}) collective-permute-start(bf16[32,2560]{1,0:T(8,128)(2,1)S(1)} %pad_maximum_fusion.11), channel_id=1, source_target_pairs={{0,96},{8,104},{16,112},{24,120},{32,0},{40,8},{48,16},{56,24},{64... | collective-permute-start | bytes 491528 | tf_op jit(solution)/shard_map/ppermute | solution.py:26
  235.1 9.6 %collective-permute-start.23 = (bf16[32,2560]{1,0:T(8,128)(2,1)S(1)}, bf16[32,2560]{1,0:T(8,128)(2,1)S(1)}, u32[]{:S(2)}, u32[]{:S(2)}) collective-permute-start(bf16[32,2560]{1,0:T(8,128)(2,1)S(1)} %pad_maximum_fusion.12), channel_id=1, source_target_pairs={{0,8},{8,16},{16,24},{24,0},{32,40},{40,48},{48,56},{56,32},{64,72... | collective-permute-start | bytes 491528 | tf_op jit(solution)/shard_map/ppermute | solution.py:26
  235.3 9.4 %collective-permute-start.25 = (bf16[32,2560]{1,0:T(8,128)(2,1)S(1)}, bf16[32,2560]{1,0:T(8,128)(2,1)S(1)}, u32[]{:S(2)}, u32[]{:S(2)}) collective-permute-start(bf16[32,2560]{1,0:T(8,128)(2,1)S(1)} %pad_maximum_fusion.13), channel_id=1, source_target_pairs={{0,24},{8,0},{16,8},{24,16},{32,56},{40,32},{48,40},{56,48},{64,88... | collective-permute-start | bytes 491528 | tf_op jit(solution)/shard_map/ppermute | solution.py:26
Sparse Core Ops, SparseCore 0:
  11.8 114.5 all-gather.1
  141.8 106.9 reduce-scatter.1
where the time goes:
time: 259 us; the launch traced here: 258 us
  waiting for transfers between devices  106 us (41%)
  local copies, waits for them, and re-layouts  40.7 us (16%)
  starting transfers between devices  37.6 us (15%)
  other arithmetic  29.5 us (11%)
  matrix products  29.4 us (11%)
  between operations  14.8 us (6%)
    all_gather x1, waiting for transfers between devices, on_device(): gathered = lax.all_gather(first_cols, 'prow', axis=1, tiled=True)  44.8 us
    ppermute x16, waiting for transfers between devices, grid_shift(): return lax.ppermute(value, axis, pairs)  29.7 us
    unnamed x44, local copies, waits for them, and re-layouts  26.8 us
    ppermute x8, waiting for transfers between devices, ring(): lax.ppermute(value, axis, [(i, (i + step) % size) for i in range(size)])  26.3 us
    ppermute x16, starting transfers between devices, grid_shift(): return lax.ppermute(value, axis, pairs)  23.2 us
    dot_general x1, matrix products, on_device(): jnp.dot(multipliers, gathered.reshape(2 * block_size, half), preferred_el...  13.9 us
    mul x1, other arithmetic, on_device(): front[0]  12.2 us
    ppermute x8, starting transfers between devices, ring(): lax.ppermute(value, axis, [(i, (i + step) % size) for i in range(size)])  11.7 us
  transfers between devices with their start and end apart: 28, of which 14 were waited for; matrix products, arithmetic and copies ran while one was open for 33% of the time, Pallas kernels for 0%

commit v1 on v0

--- a/solution.py
+++ b/solution.py
@@ -105,7 +105,9 @@
     assert n_prow == 4
     half = col_count * 11 // 16 // block_size * block_size
     first_cols = mask_pivots(0, half)
-    gathered = lax.all_gather(first_cols, "prow", axis=1, tiled=True)
+    gathered = jnp.concatenate(
+        lax.all_to_all(jnp.stack([first_cols] * lax.axis_size("prow")), "prow", 0, 0), axis=1
+    )
     later_cols, gathered = lax.optimization_barrier((mask_pivots(half, col_count), gathered))
     panel = jnp.roll(
         gather_relative(first_cols[:, :, :panel_width], "prow", n_prow), row_offset, axis=1

time: 259 us -> 315 us (1.22)
  waiting for transfers between devices: 106 us -> 140 us
  local copies, waits for them, and re-layouts: 40.7 us -> 52.8 us
  starting transfers between devices: 37.6 us -> 43.6 us
    ppermute x8, waiting for transfers between devices: 26.3 us -> 104 us  [ring(): lax.ppermute(value, axis, [(i, (i + step) % size) for i in range(size)])]
    all_gather x1 -> x0, waiting for transfers between devices: 44.8 us -> none  [on_device(): gathered = lax.all_gather(first_cols, 'prow', axis=1, tiled=True)]
    all_to_all x0 -> x1, local copies, waits for them, and re-layouts: none -> 9.97 us  [on_device(): lax.all_to_all(jnp.stack([first_cols] * lax.axis_size('prow')), 'prow', 0...]
    all_to_all x0 -> x1, starting transfers between devices: none -> 6.41 us  [on_device(): lax.all_to_all(jnp.stack([first_cols] * lax.axis_size('prow')), 'prow', 0...]
    another operation x0 -> x1, local copies, waits for them, and re-layouts: none -> 5.59 us  [on_device(): jnp.stack([first_cols] * lax.axis_size('prow'))]
    slice x0 -> x1, other arithmetic: none -> 3.94 us  [mask_pivots(): pivots[0, :, :, lo:hi]]
    mul x2 -> x1, other arithmetic: 6.1 us -> 2.48 us  [mask_pivots(): pivots[0, :, :, lo:hi]]
    unnamed x44 -> x46, local copies, waits for them, and re-layouts: 26.8 us -> 25 us
  transfers between devices with their start and end apart: 28 -> 28, of which waited for: 14 -> 14; matrix products, arithmetic and copies ran while one was open for 33% -> 29% of each run, Pallas kernels for 0% -> 0%
where the time goes in v1:
time: 315 us; the launch traced here: 314 us
  waiting for transfers between devices  140 us (44%)
  local copies, waits for them, and re-layouts  52.8 us (17%)
  starting transfers between devices  43.6 us (14%)
  matrix products  32.4 us (10%)
  other arithmetic  30.3 us (10%)
  between operations  14.9 us (5%)
    ppermute x8, waiting for transfers between devices, ring(): lax.ppermute(value, axis, [(i, (i + step) % size) for i in range(size)])  104 us
    ppermute x16, waiting for transfers between devices, grid_shift(): return lax.ppermute(value, axis, pairs)  28.8 us
    unnamed x46, local copies, waits for them, and re-layouts  25 us
    ppermute x16, starting transfers between devices, grid_shift(): return lax.ppermute(value, axis, pairs)  22.9 us
    dot_general x1, matrix products, on_device(): jnp.dot(multipliers, gathered.reshape(2 * block_size, half), preferred_el...  15.9 us
    mul x1, other arithmetic, on_device(): front[0]  12.1 us
    ppermute x8, starting transfers between devices, ring(): lax.ppermute(value, axis, [(i, (i + step) % size) for i in range(size)])  11.7 us
    all_to_all x1, local copies, waits for them, and re-layouts, on_device(): lax.all_to_all(jnp.stack([first_cols] * lax.axis_size('prow')), 'prow', 0...  9.97 us
  transfers between devices with their start and end apart: 28, of which 14 were waited for; matrix products, arithmetic and copies ran while one was open for 29% of the time, Pallas kernels for 0%

profile of v1, /device:TPU:1, one launch (start us, length us, event | category | flops | bytes accessed | tf_op | source)
XLA Modules:
  0.0 313.6 jit_solution(9358122784894011656)
XLA Ops:
  8.0 3.9 %fusion.61 = (bf16[1,2,64,11264]{3,2,1,0:T(8,128)(2,1)}, bf16[2,64,11264]{2,1,0:T(8,128)(2,1)S(1)}, bf16[2,64,11264]{2,1,0:T(8,128)(2,1)S(1)}) fusion(bf16[1,2,64,16384]{3,2,1,0:T(8,128)(2,1)} %param.8, bf16[2,11264]{1,0:T(2,128)(2,1)S(1)} %bitcast.184), kind=kLoop, calls=%fused_computation.153 | loop fusion | flops 1441792 | bytes 11579392 | tf_op jit(solution)/shard_map/slice | solution.py:93
  11.9 0.7 constant_dynamic-update-slice_fusion.9
  12.6 4.6 %collective-permute-start = (bf16[2,64,512]{2,1,0:T(8,128)(2,1)S(1)}, bf16[2,64,512]{2,1,0:T(8,128)(2,1)S(1)}, u32[]{:S(2)}, u32[]{:S(2)}) collective-permute-start(bf16[2,64,512]{2,1,0:T(8,128)(2,1)S(1)} %get-tuple-element.18), channel_id=1, source_target_pairs={{0,6},{2,0},{4,2},{6,4},{1,7},{3,1},{5,3},{7,5},{8,14},{10,8},{12,... | collective-permute-start | bytes 393224 | tf_op jit(solution)/shard_map/ppermute | solution.py:8
  17.2 5.6 %stack.3 = bf16[4,2,64,11264]{3,2,1,0:T(8,128)(2,1)} broadcast(bf16[2,64,11264]{2,1,0:T(8,128)(2,1)S(1)} %get-tuple-element.27), dimensions={1,2,3} | broadcast | bytes 14417920 | tf_op jit(solution)/shard_map/stack | solution.py:109
  22.8 6.4 %all-to-all-start = ((bf16[4,2,64,11264]{3,2,1,0:T(8,128)(2,1)}), bf16[4,2,64,11264]{3,2,1,0:T(8,128)(2,1)}, u32[]{:S(2)}, u32[]{:S(2)}) async-start(bf16[4,2,64,11264]{3,2,1,0:T(8,128)(2,1)} %stack.3), calls=%async_computation | async-start | bytes 23068672 | tf_op jit(solution)/shard_map/all_to_all | solution.py:109
  29.6 3.0 reshape_squeeze.14
  32.6 1.7 fusion.6
  34.3 1.6 copy.24
  36.0 2.7 mul.53
  38.7 12.4 %copy.22 = bf16[64,8,64,256]{3,1,2,0:T(8,128)(2,1)} copy(bf16[64,8,64,256]{3,2,1,0:T(8,128)(2,1)S(1)} %bitcast.168) | data formatting | bytes 33554432
  51.3 2.5 bitcast_multiply_fusion.1
  53.7 12.1 %bitcast_multiply_fusion = bf16[512,16384]{1,0:T(8,128)(2,1)S(1)} fusion(bf16[512,16384]{1,0:T(8,128)(2,1)} %bitcast.167, bf16[1,512,16384]{2,1,0:T(8,128)(2,1)} %param.7), kind=kLoop, calls=%fused_computation.1 | loop fusion | flops 8388608 | bytes 50331648 | tf_op jit(solution)/shard_map/mul | solution.py:87
  65.8 5.8 %copy-done = bf16[512,16384]{1,0:T(8,128)(2,1)} copy-done((bf16[512,16384]{1,0:T(8,128)(2,1)}, bf16[512,16384]{1,0:T(8,128)(2,1)S(1)}, u32[]{:S(2)}) %copy-start) | copy-done | bytes 16777240
  71.9 1.4 collective-permute-start.2
  73.3 1.4 collective-permute-start.3
  74.7 79.0 %collective-permute-done.2 = bf16[2,32,512]{2,1,0:T(8,128)(2,1)S(1)} collective-permute-done((bf16[2,32,512]{2,1,0:T(8,128)(2,1)S(1)}, bf16[2,32,512]{2,1,0:T(8,128)(2,1)S(1)}, u32[]{:S(2)}, u32[]{:S(2)}) %collective-permute-start.2) | collective-permute-done | bytes 65568 | tf_op jit(solution)/shard_map/ppermute | solution.py:8
  153.8 2.0 collective-permute-done.3
  155.9 0.7 dynamic-slice_bitcast_fusion.4
  156.8 1.3 collective-permute-start.5
  158.1 1.5 convolution_convert_fusion
  159.7 1.3 collective-permute-start.4
  162.0 0.9 broadcast_select_fusion.1
  163.6 2.4 collective-permute-done.4
  166.0 1.2 broadcast_select_fusion
  167.1 0.7 slice.342
  167.8 1.0 copy.17
  168.8 1.9 subtract_convert_fusion
  170.7 10.0 %copy.13 = bf16[4,2,64,11264]{3,2,0,1:T(8,128)(2,1)} copy(bf16[4,2,64,11264]{3,2,1,0:T(8,128)(2,1)} %all-to-all-done) | data formatting | bytes 23068672 | tf_op jit(solution)/shard_map/all_to_all | solution.py:109
  181.3 0.8 collective-permute-start.7
  182.2 15.9 %select_convert_fusion = bf16[512,11264]{1,0:T(8,128)(2,1)} fusion(bf16[512,11264]{1,0:T(8,128)(2,1)} %bitcast.169, bf16[512,16384]{1,0:T(8,128)(2,1)} %copy-done, pred[11264]{0:T(1024)(128)(4,1)S(1)} %slice-done, bf16[512,256]{0,1:T(8,128)(2,1)S(1)} %copy-done.3, bf16[512,256]{0,1:T(8,128)(2,1)S(1)} %copy-done.7), kind=kOutput, calls=%fused_computation | convolution fusion | flops 5929697280 | bytes 35138560 | tf_op jit(solution)/shard_map/dot_general | solution.py:152
  198.1 1.4 fusion.25
  199.5 1.4 constant_dynamic-update-slice_fusion.14
  200.9 11.9 %collective-permute-done.7 = bf16[2,64,5120]{2,1,0:T(8,128)(2,1)} collective-permute-done((bf16[2,64,5120]{2,1,0:T(8,128)(2,1)}, bf16[2,64,5120]{2,1,0:T(8,128)(2,1)}, u32[]{:S(2)}, u32[]{:S(2)}) %collective-permute-start.7) | collective-permute-done | bytes 1310752 | tf_op jit(solution)/shard_map/ppermute | solution.py:8
  212.8 1.1 slice.346
  214.0 3.9 %fusion = bf16[64,11264]{1,0:T(8,128)(2,1)S(1)} fusion(f32[64,11264]{1,0:T(8,128)S(1)} %bitcast.172, bf16[64,256]{1,0:T(8,128)(2,1)S(1)} %constant_dynamic-slice_fusion, bf16[2,256,11264]{2,1,0:T(8,128)(2,1)} %bitcast.170), kind=kOutput, calls=%fused_computation.3 | convolution fusion | flops 370540544 | bytes 10125312 | tf_op jit(solution)/shard_map/dot_general | solution.py:167
  217.9 1.1 slice.347
  219.0 2.7 collective-permute-start.9
  221.8 1.5 constant_dynamic-update-slice_fusion.13
  223.3 7.0 %collective-permute-done.8 = bf16[2,32,5120]{2,1,0:T(8,128)(2,1)S(1)} collective-permute-done((bf16[2,32,5120]{2,1,0:T(8,128)(2,1)S(1)}, bf16[2,32,5120]{2,1,0:T(8,128)(2,1)S(1)}, u32[]{:S(2)}, u32[]{:S(2)}) %collective-permute-start.8) | collective-permute-done | bytes 655392 | tf_op jit(solution)/shard_map/ppermute | solution.py:8
  230.3 3.9 %collective-permute-done.9 = bf16[2,32,5120]{2,1,0:T(8,128)(2,1)S(1)} collective-permute-done((bf16[2,32,5120]{2,1,0:T(8,128)(2,1)S(1)}, bf16[2,32,5120]{2,1,0:T(8,128)(2,1)S(1)}, u32[]{:S(2)}, u32[]{:S(2)}) %collective-permute-start.9) | collective-permute-done | bytes 655392 | tf_op jit(solution)/shard_map/ppermute | solution.py:8
  234.3 1.5 constant_dynamic-update-slice_fusion.10
  235.9 3.6 %subtract_select_fusion.1 = f32[512,2560]{1,0:T(8,128)S(1)} fusion(bf16[512,5120]{1,0:T(8,128)(2,1)S(1)} %bitcast.181, bf16[512,16384]{1,0:T(8,128)(2,1)} %copy-done, pred[2560]{0:T(1024)(128)(4,1)S(1)} %copy-done.11, bf16[512,256]{0,1:T(8,128)(2,1)S(1)} %get-tuple-element.48, bf16[512,256]{0,1:T(8,128)(2,1)S(1)} %get-tuple-element.49), kind=kOutput, calls=%fused_computation.9 | convolution fusion | flops 1347158016 | bytes 11013120 | tf_op jit(solution)/shard_map/dot_general | solution.py:185
  239.6 1.0 collective-permute-start.10
  240.6 1.7 collective-permute-start.12
  242.3 3.4 %subtract_select_fusion = f32[512,2560]{1,0:T(8,128)S(1)} fusion(bf16[512,5120]{1,0:T(8,128)(2,1)S(1)} %bitcast.182, bf16[512,16384]{1,0:T(8,128)(2,1)} %copy-done, pred[2560]{0:T(1024)(128)(4,1)S(1)} %copy-done.10, bf16[512,256]{0,1:T(8,128)(2,1)S(1)} %get-tuple-element.48, bf16[512,256]{0,1:T(8,128)(2,1)S(1)} %get-tuple-element.49), kind=kOutput, calls=%fused_computation.8 | convolution fusion | flops 1347158016 | bytes 11013120 | tf_op jit(solution)/shard_map/dot_general | solution.py:185
  245.9 1.1 collective-permute-start.18
  247.0 1.6 collective-permute-start.20
  248.6 1.8 fusion.1
  250.7 1.5 maximum_bitcast_fusion.1
  252.3 4.3 %collective-permute-done.10 = bf16[2,32,2560]{2,1,0:T(8,128)(2,1)S(1)} collective-permute-done((bf16[2,32,2560]{2,1,0:T(8,128)(2,1)S(1)}, bf16[2,32,2560]{2,1,0:T(8,128)(2,1)S(1)}, u32[]{:S(2)}, u32[]{:S(2)}) %collective-permute-start.10) | collective-permute-done | bytes 327712 | tf_op jit(solution)/shard_map/ppermute | solution.py:26
  257.1 2.7 collective-permute-start.13
  259.9 0.9 collective-permute-done.18
  260.9 0.9 collective-permute-start.19
  261.9 1.9 collective-permute-start.21
  263.8 16.9 %collective-permute-done.11 = bf16[4,32,2560]{2,1,0:T(8,128)(2,1)S(1)} collective-permute-done((bf16[4,32,2560]{2,1,0:T(8,128)(2,1)S(1)}, bf16[4,32,2560]{2,1,0:T(8,128)(2,1)S(1)}, u32[]{:S(2)}, u32[]{:S(2)}) %collective-permute-start.11) | collective-permute-done | bytes 655392 | tf_op jit(solution)/shard_map/ppermute | solution.py:26
  281.0 2.7 collective-permute-start.16
  284.4 2.4 collective-permute-start.24
  287.0 3.2 %collective-permute-start.17 = (bf16[32,2560]{1,0:T(8,128)(2,1)S(1)}, bf16[32,2560]{1,0:T(8,128)(2,1)S(1)}, u32[]{:S(2)}, u32[]{:S(2)}) collective-permute-start(bf16[32,2560]{1,0:T(8,128)(2,1)S(1)} %pad_maximum_fusion.11), channel_id=1, source_target_pairs={{0,96},{8,104},{16,112},{24,120},{32,0},{40,8},{48,16},{56,24},{64... | collective-permute-start | bytes 491528 | tf_op jit(solution)/shard_map/ppermute | solution.py:26
  290.8 2.7 collective-permute-start.25
  293.5 3.2 %collective-permute-done.15 = bf16[32,2560]{1,0:T(8,128)(2,1)S(1)} collective-permute-done((bf16[32,2560]{1,0:T(8,128)(2,1)S(1)}, bf16[32,2560]{1,0:T(8,128)(2,1)S(1)}, u32[]{:S(2)}, u32[]{:S(2)}) %collective-permute-start.15) | collective-permute-done | bytes 163872 | tf_op jit(solution)/shard_map/ppermute | solution.py:26
  296.7 3.2 %collective-permute-done.23 = bf16[32,2560]{1,0:T(8,128)(2,1)S(1)} collective-permute-done((bf16[32,2560]{1,0:T(8,128)(2,1)S(1)}, bf16[32,2560]{1,0:T(8,128)(2,1)S(1)}, u32[]{:S(2)}, u32[]{:S(2)}) %collective-permute-start.23) | collective-permute-done | bytes 163872 | tf_op jit(solution)/shard_map/ppermute | solution.py:26
  300.0 4.1 %reduce-scatter.2.cloned.1.call-done = bf16[32,11264]{1,0:T(8,128)(2,1)} async-done(((bf16[512,11264]{1,0:T(8,128)(2,1)}), bf16[32,11264]{1,0:T(8,128)(2,1)}) %reduce-scatter.2.cloned.1.call-update) | async-done | bytes 720912 | tf_op jit(solution)/shard_map/reduce_scatter | solution.py:158
  304.1 1.2 convert_element_type.165
  305.3 1.5 maximum_bitcast_fusion
  (113 shorter events, 7.2 us)
Async XLA Ops:
  12.6 60.7 %collective-permute-start = (bf16[2,64,512]{2,1,0:T(8,128)(2,1)S(1)}, bf16[2,64,512]{2,1,0:T(8,128)(2,1)S(1)}, u32[]{:S(2)}, u32[]{:S(2)}) collective-permute-start(bf16[2,64,512]{2,1,0:T(8,128)(2,1)S(1)} %get-tuple-element.18), channel_id=1, source_target_pairs={{0,6},{2,0},{4,2},{6,4},{1,7},{3,1},{5,3},{7,5},{8,14},{10,8},{12,... | collective-permute-start | bytes 393224 | tf_op jit(solution)/shard_map/ppermute | solution.py:8
  17.2 54.7 %collective-permute-start.1 = (bf16[2,64,512]{2,1,0:T(8,128)(2,1)S(1)}, bf16[2,64,512]{2,1,0:T(8,128)(2,1)S(1)}, u32[]{:S(2)}, u32[]{:S(2)}) collective-permute-start(bf16[2,64,512]{2,1,0:T(8,128)(2,1)S(1)} %get-tuple-element.18), channel_id=1, source_target_pairs={{0,2},{2,4},{4,6},{6,0},{1,3},{3,5},{5,7},{7,1},{8,10},{10,12},{12... | collective-permute-start | bytes 393224 | tf_op jit(solution)/shard_map/ppermute | solution.py:8
  22.8 6.8 %copy-start.1 = (bf16[1,2,64,11264]{3,2,1,0:T(8,128)(2,1)S(1)}, bf16[1,2,64,11264]{3,2,1,0:T(8,128)(2,1)}, u32[]{:S(2)}) copy-start(bf16[1,2,64,11264]{3,2,1,0:T(8,128)(2,1)} %get-tuple-element.25) | copy-start | bytes 8650756
  22.8 147.9 %all-to-all-start = ((bf16[4,2,64,11264]{3,2,1,0:T(8,128)(2,1)}), bf16[4,2,64,11264]{3,2,1,0:T(8,128)(2,1)}, u32[]{:S(2)}, u32[]{:S(2)}) async-start(bf16[4,2,64,11264]{3,2,1,0:T(8,128)(2,1)} %stack.3), calls=%async_computation | async-start | bytes 23068672 | tf_op jit(solution)/shard_map/all_to_all | solution.py:109
  29.2 274.9 %reduce-scatter.2.cloned.1.call-start = ((), (), s32[]{:S(2)}) async-start(), calls=%async_computation.2 | async-start | bytes 12255232 | tf_op jit(solution)/shard_map/reduce_scatter | solution.py:158
  34.3 1.7 copy-start.12
  51.2 109.8 %copy-start.9 = (pred[16384]{0:T(1024)(128)(4,1)}, pred[16384]{0:T(1024)(128)(4,1)S(1)}, u32[]{:S(2)}) copy-start(pred[16384]{0:T(1024)(128)(4,1)S(1)} %add_compare_fusion) | copy-start | bytes 49156
  53.7 17.9 %copy-start.6 = (bf16[1,2,256,256]{3,2,1,0:T(8,128)(2,1)S(1)}, bf16[1,2,256,256]{3,2,1,0:T(8,128)(2,1)}, u32[]{:S(2)}) copy-start(bf16[1,2,256,256]{3,2,1,0:T(8,128)(2,1)} %param.9) | copy-start | bytes 786436
  53.7 21.0 %copy-start.5 = (bf16[2,512,512]{2,1,0:T(8,128)(2,1)S(1)}, bf16[2,512,512]{2,1,0:T(8,128)(2,1)}, u32[]{:S(2)}) copy-start(bf16[2,512,512]{2,1,0:T(8,128)(2,1)} %get-tuple-element.17) | copy-start | bytes 3145732
  65.8 5.8 %copy-start = (bf16[512,16384]{1,0:T(8,128)(2,1)}, bf16[512,16384]{1,0:T(8,128)(2,1)S(1)}, u32[]{:S(2)}) copy-start(bf16[512,16384]{1,0:T(8,128)(2,1)S(1)} %bitcast_multiply_fusion) | copy-start | bytes 50331652
  71.9 91.1 %copy-start.2 = (bf16[512,256]{0,1:T(8,128)(2,1)}, bf16[512,256]{0,1:T(8,128)(2,1)S(1)}, u32[]{:S(2)}) copy-start(bf16[512,256]{0,1:T(8,128)(2,1)S(1)} %convolution_convert_fusion.1) | copy-start | bytes 786436
  71.9 81.9 %collective-permute-start.2 = (bf16[2,32,512]{2,1,0:T(8,128)(2,1)S(1)}, bf16[2,32,512]{2,1,0:T(8,128)(2,1)S(1)}, u32[]{:S(2)}, u32[]{:S(2)}) collective-permute-start(bf16[2,32,512]{2,1,0:T(8,128)(2,1)S(1)} %slice.338), channel_id=1, source_target_pairs={{0,2},{2,4},{4,6},{6,0},{1,3},{3,5},{5,7},{7,1},{8,10},{10,12},{12... | collective-permute-start | bytes 196616 | tf_op jit(solution)/shard_map/ppermute | solution.py:8
  73.3 82.4 %collective-permute-start.3 = (bf16[2,32,512]{2,1,0:T(8,128)(2,1)S(1)}, bf16[2,32,512]{2,1,0:T(8,128)(2,1)S(1)}, u32[]{:S(2)}, u32[]{:S(2)}) collective-permute-start(bf16[2,32,512]{2,1,0:T(8,128)(2,1)S(1)} %slice.339), channel_id=1, source_target_pairs={{0,6},{2,0},{4,2},{6,4},{1,7},{3,1},{5,3},{7,5},{8,14},{10,8},{12,... | collective-permute-start | bytes 196616 | tf_op jit(solution)/shard_map/ppermute | solution.py:8
  156.8 5.2 %collective-permute-start.5 = (bf16[256,256]{1,0:T(8,128)(2,1)S(1)}, bf16[256,256]{1,0:T(8,128)(2,1)}, u32[]{:S(2)}, u32[]{:S(2)}) collective-permute-start(bf16[256,256]{1,0:T(8,128)(2,1)S(1)} %convolution_convert_fusion.2), channel_id=1, source_target_pairs={{0,1},{2,3},{4,5},{6,7},{8,9},{10,11},{12,13},{14,15},{16,17},{18,... | collective-permute-start | bytes 393224 | tf_op jit(solution)/shard_map/ppermute | solution.py:134
  159.6 3.3 %copy-start.4 = (bf16[512,256]{0,1:T(8,128)(2,1)}, bf16[512,256]{0,1:T(8,128)(2,1)S(1)}, u32[]{:S(2)}) copy-start(bf16[512,256]{0,1:T(8,128)(2,1)S(1)} %convolution_convert_fusion) | copy-start | bytes 786436
  159.7 6.3 %collective-permute-start.4 = (bf16[512,512]{0,1:T(8,128)(2,1)S(1)}, bf16[512,512]{0,1:T(8,128)(2,1)S(1)}, u32[]{:S(2)}, u32[]{:S(2)}) collective-permute-start(bf16[512,512]{0,1:T(8,128)(2,1)S(1)} %pad_maximum_fusion.6), channel_id=1, source_target_pairs={{0,1},{2,3},{4,5},{6,7},{8,9},{10,11},{12,13},{14,15},{16,17},{18,... | collective-permute-start | bytes 1572872 | tf_op jit(solution)/shard_map/ppermute | solution.py:134
  162.9 0.6 copy-start.8
  170.7 11.4 %copy-start.3 = (bf16[512,256]{0,1:T(8,128)(2,1)S(1)}, bf16[512,256]{0,1:T(8,128)(2,1)}, u32[]{:S(2)}) copy-start(bf16[512,256]{0,1:T(8,128)(2,1)} %slice.342) | copy-start | bytes 786436
  170.7 11.4 %copy-start.7 = (bf16[512,256]{0,1:T(8,128)(2,1)S(1)}, bf16[512,256]{0,1:T(8,128)(2,1)}, u32[]{:S(2)}) copy-start(bf16[512,256]{0,1:T(8,128)(2,1)} %subtract_convert_fusion) | copy-start | bytes 786436
  170.7 11.4 %slice-start = ((pred[16384]{0:T(1024)(128)(4,1)}), pred[11264]{0:T(1024)(128)(4,1)S(1)}, s32[]{:S(2)}) async-start(pred[16384]{0:T(1024)(128)(4,1)} %copy-done.9), calls=%async_computation.3 | async-start | bytes 22528 | tf_op jit(solution)/shard_map/slice | solution.py:155
  180.7 37.2 %collective-permute-start.6 = (bf16[2,64,5120]{2,1,0:T(8,128)(2,1)}, bf16[2,64,5120]{2,1,0:T(8,128)(2,1)}, u32[]{:S(2)}, u32[]{:S(2)}) collective-permute-start(bf16[2,64,5120]{2,1,0:T(8,128)(2,1)} %bitcast_multiply_fusion.1), channel_id=1, source_target_pairs={{0,6},{2,0},{4,2},{6,4},{1,7},{3,1},{5,3},{7,5},{8,14},{10,8},{12,... | collective-permute-start | bytes 3932168 | tf_op jit(solution)/shard_map/ppermute | solution.py:8
  181.3 31.4 %collective-permute-start.7 = (bf16[2,64,5120]{2,1,0:T(8,128)(2,1)}, bf16[2,64,5120]{2,1,0:T(8,128)(2,1)}, u32[]{:S(2)}, u32[]{:S(2)}) collective-permute-start(bf16[2,64,5120]{2,1,0:T(8,128)(2,1)} %bitcast_multiply_fusion.1), channel_id=1, source_target_pairs={{0,2},{2,4},{4,6},{6,0},{1,3},{3,5},{5,7},{7,1},{8,10},{10,12},{12... | collective-permute-start | bytes 3932168 | tf_op jit(solution)/shard_map/ppermute | solution.py:8
  213.9 16.3 %collective-permute-start.8 = (bf16[2,32,5120]{2,1,0:T(8,128)(2,1)S(1)}, bf16[2,32,5120]{2,1,0:T(8,128)(2,1)S(1)}, u32[]{:S(2)}, u32[]{:S(2)}) collective-permute-start(bf16[2,32,5120]{2,1,0:T(8,128)(2,1)S(1)} %slice.346), channel_id=1, source_target_pairs={{0,2},{2,4},{4,6},{6,0},{1,3},{3,5},{5,7},{7,1},{8,10},{10,12},{12... | collective-permute-start | bytes 1966088 | tf_op jit(solution)/shard_map/ppermute | solution.py:8
  219.0 15.2 %collective-permute-start.9 = (bf16[2,32,5120]{2,1,0:T(8,128)(2,1)S(1)}, bf16[2,32,5120]{2,1,0:T(8,128)(2,1)S(1)}, u32[]{:S(2)}, u32[]{:S(2)}) collective-permute-start(bf16[2,32,5120]{2,1,0:T(8,128)(2,1)S(1)} %slice.347), channel_id=1, source_target_pairs={{0,6},{2,0},{4,2},{6,4},{1,7},{3,1},{5,3},{7,5},{8,14},{10,8},{12,... | collective-permute-start | bytes 1966088 | tf_op jit(solution)/shard_map/ppermute | solution.py:8
  223.3 12.6 %copy-start.11 = (pred[2560]{0:T(1024)(128)(4,1)S(1)}, pred[2560]{0:T(1024)(128)(4,1)}, u32[]{:S(2)}) copy-start(pred[2560]{0:T(1024)(128)(4,1)} %get-tuple-element.46) | copy-start | bytes 7684
  235.8 6.5 %copy-start.10 = (pred[2560]{0:T(1024)(128)(4,1)S(1)}, pred[2560]{0:T(1024)(128)(4,1)}, u32[]{:S(2)}) copy-start(pred[2560]{0:T(1024)(128)(4,1)} %get-tuple-element.47) | copy-start | bytes 7684
  239.6 16.9 %collective-permute-start.10 = (bf16[2,32,2560]{2,1,0:T(8,128)(2,1)S(1)}, bf16[2,32,2560]{2,1,0:T(8,128)(2,1)S(1)}, u32[]{:S(2)}, u32[]{:S(2)}) collective-permute-start(bf16[2,32,2560]{2,1,0:T(8,128)(2,1)S(1)} %get-tuple-element.38), channel_id=1, source_target_pairs={{0,8},{8,16},{16,24},{24,0},{32,40},{40,48},{48,56},{56,32},{64,72... | collective-permute-start | bytes 983048 | tf_op jit(solution)/shard_map/ppermute | solution.py:26
  240.6 16.3 %collective-permute-start.12 = (bf16[2,32,2560]{2,1,0:T(8,128)(2,1)S(1)}, bf16[2,32,2560]{2,1,0:T(8,128)(2,1)S(1)}, u32[]{:S(2)}, u32[]{:S(2)}) collective-permute-start(bf16[2,32,2560]{2,1,0:T(8,128)(2,1)S(1)} %get-tuple-element.39), channel_id=1, source_target_pairs={{0,24},{8,0},{16,8},{24,16},{32,56},{40,32},{48,40},{56,48},{64,88... | collective-permute-start | bytes 983048 | tf_op jit(solution)/shard_map/ppermute | solution.py:26
  245.9 14.8 %collective-permute-start.18 = (bf16[2,32,2560]{2,1,0:T(8,128)(2,1)S(1)}, bf16[2,32,2560]{2,1,0:T(8,128)(2,1)S(1)}, u32[]{:S(2)}, u32[]{:S(2)}) collective-permute-start(bf16[2,32,2560]{2,1,0:T(8,128)(2,1)S(1)} %get-tuple-element.40), channel_id=1, source_target_pairs={{0,32},{8,40},{16,48},{24,56},{32,64},{40,72},{48,80},{56,88},{64,... | collective-permute-start | bytes 983048 | tf_op jit(solution)/shard_map/ppermute | solution.py:26
  247.0 13.7 %collective-permute-start.20 = (bf16[2,32,2560]{2,1,0:T(8,128)(2,1)S(1)}, bf16[2,32,2560]{2,1,0:T(8,128)(2,1)S(1)}, u32[]{:S(2)}, u32[]{:S(2)}) collective-permute-start(bf16[2,32,2560]{2,1,0:T(8,128)(2,1)S(1)} %get-tuple-element.41), channel_id=1, source_target_pairs={{0,96},{8,104},{16,112},{24,120},{32,0},{40,8},{48,16},{56,24},{64... | collective-permute-start | bytes 983048 | tf_op jit(solution)/shard_map/ppermute | solution.py:26
  256.7 24.0 %collective-permute-start.11 = (bf16[4,32,2560]{2,1,0:T(8,128)(2,1)S(1)}, bf16[4,32,2560]{2,1,0:T(8,128)(2,1)S(1)}, u32[]{:S(2)}, u32[]{:S(2)}) collective-permute-start(bf16[4,32,2560]{2,1,0:T(8,128)(2,1)S(1)} %pad_maximum_fusion), channel_id=1, source_target_pairs={{0,8},{8,16},{16,24},{24,0},{32,40},{40,48},{48,56},{56,32},{64,72... | collective-permute-start | bytes 1966088 | tf_op jit(solution)/shard_map/ppermute | solution.py:26
  257.1 23.5 %collective-permute-start.13 = (bf16[4,32,2560]{2,1,0:T(8,128)(2,1)S(1)}, bf16[4,32,2560]{2,1,0:T(8,128)(2,1)S(1)}, u32[]{:S(2)}, u32[]{:S(2)}) collective-permute-start(bf16[4,32,2560]{2,1,0:T(8,128)(2,1)S(1)} %pad_maximum_fusion.1), channel_id=1, source_target_pairs={{0,24},{8,0},{16,8},{24,16},{32,56},{40,32},{48,40},{56,48},{64,88... | collective-permute-start | bytes 1966088 | tf_op jit(solution)/shard_map/ppermute | solution.py:26
  260.9 22.8 %collective-permute-start.19 = (bf16[4,32,2560]{2,1,0:T(8,128)(2,1)S(1)}, bf16[4,32,2560]{2,1,0:T(8,128)(2,1)S(1)}, u32[]{:S(2)}, u32[]{:S(2)}) collective-permute-start(bf16[4,32,2560]{2,1,0:T(8,128)(2,1)S(1)} %pad_maximum_fusion.2), channel_id=1, source_target_pairs={{0,32},{8,40},{16,48},{24,56},{32,64},{40,72},{48,80},{56,88},{64,... | collective-permute-start | bytes 1966088 | tf_op jit(solution)/shard_map/ppermute | solution.py:26
  261.9 21.8 %collective-permute-start.21 = (bf16[4,32,2560]{2,1,0:T(8,128)(2,1)S(1)}, bf16[4,32,2560]{2,1,0:T(8,128)(2,1)S(1)}, u32[]{:S(2)}, u32[]{:S(2)}) collective-permute-start(bf16[4,32,2560]{2,1,0:T(8,128)(2,1)S(1)} %pad_maximum_fusion.3), channel_id=1, source_target_pairs={{0,96},{8,104},{16,112},{24,120},{32,0},{40,8},{48,16},{56,24},{64... | collective-permute-start | bytes 1966088 | tf_op jit(solution)/shard_map/ppermute | solution.py:26
  280.9 5.9 %collective-permute-start.14 = (bf16[16,2560]{1,0:T(8,128)(2,1)S(1)}, bf16[16,2560]{1,0:T(8,128)(2,1)S(1)}, u32[]{:S(2)}, u32[]{:S(2)}) collective-permute-start(bf16[16,2560]{1,0:T(8,128)(2,1)S(1)} %get-tuple-element.42), channel_id=1, source_target_pairs={{0,32},{8,40},{16,48},{24,56},{32,64},{40,72},{48,80},{56,88},{64,... | collective-permute-start | bytes 245768 | tf_op jit(solution)/shard_map/ppermute | solution.py:26
  281.0 5.8 %collective-permute-start.16 = (bf16[16,2560]{1,0:T(8,128)(2,1)S(1)}, bf16[16,2560]{1,0:T(8,128)(2,1)S(1)}, u32[]{:S(2)}, u32[]{:S(2)}) collective-permute-start(bf16[16,2560]{1,0:T(8,128)(2,1)S(1)} %get-tuple-element.43), channel_id=1, source_target_pairs={{0,96},{8,104},{16,112},{24,120},{32,0},{40,8},{48,16},{56,24},{64... | collective-permute-start | bytes 245768 | tf_op jit(solution)/shard_map/ppermute | solution.py:26
  284.1 6.5 %collective-permute-start.22 = (bf16[16,2560]{1,0:T(8,128)(2,1)S(1)}, bf16[16,2560]{1,0:T(8,128)(2,1)S(1)}, u32[]{:S(2)}, u32[]{:S(2)}) collective-permute-start(bf16[16,2560]{1,0:T(8,128)(2,1)S(1)} %get-tuple-element.44), channel_id=1, source_target_pairs={{0,8},{8,16},{16,24},{24,0},{32,40},{40,48},{48,56},{56,32},{64,72... | collective-permute-start | bytes 245768 | tf_op jit(solution)/shard_map/ppermute | solution.py:26
  284.4 6.2 %collective-permute-start.24 = (bf16[16,2560]{1,0:T(8,128)(2,1)S(1)}, bf16[16,2560]{1,0:T(8,128)(2,1)S(1)}, u32[]{:S(2)}, u32[]{:S(2)}) collective-permute-start(bf16[16,2560]{1,0:T(8,128)(2,1)S(1)} %get-tuple-element.45), channel_id=1, source_target_pairs={{0,24},{8,0},{16,8},{24,16},{32,56},{40,32},{48,40},{56,48},{64,88... | collective-permute-start | bytes 245768 | tf_op jit(solution)/shard_map/ppermute | solution.py:26
  286.9 9.8 %collective-permute-start.15 = (bf16[32,2560]{1,0:T(8,128)(2,1)S(1)}, bf16[32,2560]{1,0:T(8,128)(2,1)S(1)}, u32[]{:S(2)}, u32[]{:S(2)}) collective-permute-start(bf16[32,2560]{1,0:T(8,128)(2,1)S(1)} %pad_maximum_fusion.10), channel_id=1, source_target_pairs={{0,32},{8,40},{16,48},{24,56},{32,64},{40,72},{48,80},{56,88},{64,... | collective-permute-start | bytes 491528 | tf_op jit(solution)/shard_map/ppermute | solution.py:26
  287.0 9.7 %collective-permute-start.17 = (bf16[32,2560]{1,0:T(8,128)(2,1)S(1)}, bf16[32,2560]{1,0:T(8,128)(2,1)S(1)}, u32[]{:S(2)}, u32[]{:S(2)}) collective-permute-start(bf16[32,2560]{1,0:T(8,128)(2,1)S(1)} %pad_maximum_fusion.11), channel_id=1, source_target_pairs={{0,96},{8,104},{16,112},{24,120},{32,0},{40,8},{48,16},{56,24},{64... | collective-permute-start | bytes 491528 | tf_op jit(solution)/shard_map/ppermute | solution.py:26
  290.7 9.3 %collective-permute-start.23 = (bf16[32,2560]{1,0:T(8,128)(2,1)S(1)}, bf16[32,2560]{1,0:T(8,128)(2,1)S(1)}, u32[]{:S(2)}, u32[]{:S(2)}) collective-permute-start(bf16[32,2560]{1,0:T(8,128)(2,1)S(1)} %pad_maximum_fusion.12), channel_id=1, source_target_pairs={{0,8},{8,16},{16,24},{24,0},{32,40},{40,48},{48,56},{56,32},{64,72... | collective-permute-start | bytes 491528 | tf_op jit(solution)/shard_map/ppermute | solution.py:26
  290.8 9.2 %collective-permute-start.25 = (bf16[32,2560]{1,0:T(8,128)(2,1)S(1)}, bf16[32,2560]{1,0:T(8,128)(2,1)S(1)}, u32[]{:S(2)}, u32[]{:S(2)}) collective-permute-start(bf16[32,2560]{1,0:T(8,128)(2,1)S(1)} %pad_maximum_fusion.13), channel_id=1, source_target_pairs={{0,24},{8,0},{16,8},{24,16},{32,56},{40,32},{48,40},{56,48},{64,88... | collective-permute-start | bytes 491528 | tf_op jit(solution)/shard_map/ppermute | solution.py:26
Sparse Core Ops, SparseCore 0:
  198.2 105.8 reduce-scatter.1
